TPU v7x, 256 devices: a whole 4x4x8 slice. The times are simulated.
256 devices in a mesh: rows: 8 (over y, core), cols: 8 (over z), layers: 4 (over x).
Axes of the slice: x: 4, y: 4, z: 8, core: 2. Of those that a mesh axis runs over, the one named last changes fastest.
Arguments:
- y_blocks: bfloat16 [192, 32, 128, 128], P('rows', ('cols', 'layers')), may hold values from -1 to 1
- y_cols: int32 [192, 32], P('rows', ('cols', 'layers')), may hold values from 0 to 191, as said below
- prod_blocks: bfloat16 [192, 32, 128, 128], P('rows', ('cols', 'layers')), may hold values from -1 to 1
- prod_cols: int32 [192, 32], P('rows', ('cols', 'layers')), may hold values from 0 to 191, as said below
- out_cols: int32 [192, 32, 2], P('rows', ('cols', 'layers')), may hold values from 0 to 191, as said below
Outputs:
- y_next: bfloat16 [192, 32, 2, 128, 128], P('rows', ('cols', 'layers'))
Inputs may be any that keep to these rules, and one draw needn't show every extreme that they name: y_cols[i, t] lies in [t * 6, (t + 1) * 6): each block row of Y holds exactly one block in each range of 6 block columns. prod_cols[k, t] lies in [t * 6, (t + 1) * 6): each block row of M holds exactly one block in each range of 6 block columns. out_cols[i, t, :] are 2 distinct block columns in [t * 6, (t + 1) * 6), one of them equal to y_cols[i, t].
All inputs are finite; a program needn't handle non-finite values.
Results may differ from a plain program's by a relative error of at most 0.001.
Values may be sent and summed in bfloat16 or wider, within the bound.
No kernel may reach another device: no remote copies, remote signals or barrier semaphores. Data moves between devices by JAX's collectives and lax.ppermute only.
A program may use at most 128 MiB of HBM per device.

v0:
```python
import jax
import jax.numpy as jnp
from jax import lax
from jax.sharding import PartitionSpec as P

TILE_COLS = 6


def partial_products(
    running, shard_piece, lookup, lookup_cols, target_cols, layer_count, tile_cols
):
    left_all, left_cols = shard_piece
    block_rows, piece_len = left_cols.shape
    tile_count = target_cols.shape[1]
    outputs = block_rows * tile_count
    group_size = 1
    while group_size * 2 <= max(1, 64 // outputs) and piece_len % (group_size * 2) == 0:
        group_size = group_size * 2

    def advance(position, summed):
        offset = position * group_size
        left_blocks = lax.dynamic_slice_in_dim(left_all, offset, group_size, 1)
        inner_cols = lax.dynamic_slice_in_dim(left_cols, offset, group_size, 1)
        lookup_rows = inner_cols // (layer_count * tile_cols) * tile_cols + inner_cols % tile_cols
        right_blocks = lookup[lookup_rows]
        right_cols = lookup_cols[lookup_rows]
        present = (right_cols[:, :, :, None] == target_cols[:, None, :, :]).astype(jnp.float32)
        products = jnp.einsum(
            "igab,igtbc->igtac", left_blocks, right_blocks, preferred_element_type=jnp.float32
        )
        weighted = jnp.sum(products[:, :, :, None] * present[..., None, None], axis=1)
        return summed + weighted

    return lax.fori_loop(0, piece_len // group_size, advance, running)


def shards(y_blocks, y_cols, prod_blocks, prod_cols, out_cols):
    block_rows = y_blocks.shape[0]
    block_size = y_blocks.shape[2]
    out_width = out_cols.shape[2]
    tile_cols = TILE_COLS
    lookup, lookup_cols = (
        lax.all_gather(prod_blocks, "rows", axis=0, tiled=True),
        lax.all_gather(prod_cols, "rows", axis=0, tiled=True),
    )
    initial = jnp.zeros((block_rows, 1, out_width, block_size, block_size), jnp.float32)
    summed = partial_products(
        initial,
        (
            lax.all_gather(y_blocks, ("cols", "layers"), axis=1, tiled=True),
            lax.all_gather(y_cols, ("cols", "layers"), axis=1, tiled=True),
        ),
        lookup,
        lookup_cols,
        out_cols,
        1,
        tile_cols,
    )
    matches = out_cols == y_cols[:, :, None]
    own_blocks = jnp.where(matches[..., None, None], y_blocks[:, :, None].astype(jnp.float32), 0.0)
    updated = 1.5 * own_blocks - 0.5 * summed
    return updated.astype(jnp.bfloat16)


def solution(mesh):
    placed = (
        P("rows", ("cols", "layers"), None, None),
        P("rows", ("cols", "layers")),
        P("rows", ("cols", "layers"), None, None),
        P("rows", ("cols", "layers")),
        P("rows", ("cols", "layers"), None),
    )
    return jax.shard_map(
        shards,
        mesh=mesh,
        in_specs=placed,
        out_specs=P("rows", ("cols", "layers"), None, None, None),
        check_vma=False,
    )
```

profile of v0, /device:TPU:1, one launch (start us, length us, event | category | flops | bytes accessed | tf_op | source)
XLA Modules:
  0.0 567.5 jit_solution(7262077693090824826)
XLA Ops:
  10.6 36.9 %all-gather = s32[32,1,24]{2,1,0:T(1,128)S(1)} all-gather(s32[1,1,24]{2,1,0:T(1,128)} %bitcast.54), channel_id=1, replica_groups=mesh['rows'=8,'cols'=8,'layers'=4] {'cols','layers'}, dimensions={0}, use_global_device_ids=true | all-gather | bytes 3168 | tf_op jit(solution)/shard_map/all_gather | solution.py:51
  48.3 13.6 %all-reduce = s32[192]{0:T(256)S(1)} all-reduce(s32[192]{0:T(256)S(1)} %bitcast_dynamic-update-slice_fusion), channel_id=1, replica_groups=mesh['rows'=8,'cols'=8,'layers'=4] {'rows'}, use_global_device_ids=true, to_apply=%add | all-reduce | flops 192 | bytes 1536
  64.4 177.4 %all-gather.6.cloned.1.call-done = bf16[24,32,128,128]{3,2,1,0:T(8,128)(2,1)} async-done(((bf16[24,1,128,128]{3,2,1,0:T(8,128)(2,1)}), bf16[24,32,128,128]{3,2,1,0:T(8,128)(2,1)}) %all-gather.6.cloned.1.call-update) | async-done | bytes 25165840 | tf_op jit(solution)/shard_map/all_gather | solution.py:50
  241.8 314.7 %while.16 = (s32[]{:T(128)}, f32[24,1,2,128,128]{4,3,2,0,1:T(8,128)}, s32[24,32]{0,1:T(8,128)S(1)}, bf16[192,1,128,128]{3,2,1,0:T(8,128)(2,1)}, bf16[24,32,128,1...) while((s32[]{:T(128)}, ...), condition=%wide.region_2.3_spmd.clone, body=%wide.region_0.2_spmd.clone.sunk | while | flops 205260784 | bytes 31465964 | solution.py:34
  242.1 3.6 gather_fusion.1
  245.7 4.4 convolution_bitcast_fusion.2
  256.3 4.3 bitcast_add_fusion.2
  260.8 3.6 gather_fusion.1
  264.5 4.4 convolution_bitcast_fusion.2
  275.0 5.3 bitcast_add_fusion.2
  280.6 3.6 gather_fusion.1
  284.2 4.4 convolution_bitcast_fusion.2
  294.8 5.3 bitcast_add_fusion.2
  300.3 3.6 gather_fusion.1
  303.9 4.4 convolution_bitcast_fusion.2
  314.5 5.3 bitcast_add_fusion.2
  320.0 3.6 gather_fusion.1
  323.7 4.4 convolution_bitcast_fusion.2
  334.2 5.3 bitcast_add_fusion.2
  339.7 3.6 gather_fusion.1
  343.4 4.4 convolution_bitcast_fusion.2
  353.9 5.3 bitcast_add_fusion.2
  363.1 4.4 convolution_bitcast_fusion.2
  373.7 5.3 bitcast_add_fusion.2
  382.8 4.4 convolution_bitcast_fusion.2
  393.4 5.3 bitcast_add_fusion.2
  402.6 4.4 convolution_bitcast_fusion.2
  413.1 5.3 bitcast_add_fusion.2
  422.3 4.4 convolution_bitcast_fusion.2
  432.9 5.3 bitcast_add_fusion.2
  438.4 3.6 gather_fusion.1
  442.0 4.4 convolution_bitcast_fusion.2
  452.6 5.3 bitcast_add_fusion.2
  458.1 3.6 gather_fusion.1
  461.7 4.4 convolution_bitcast_fusion.2
  472.3 5.3 bitcast_add_fusion.2
  481.5 4.4 convolution_bitcast_fusion.2
  492.0 5.3 bitcast_add_fusion.2
  497.6 3.6 gather_fusion.1
  501.2 4.4 convolution_bitcast_fusion.2
  511.8 5.3 bitcast_add_fusion.2
  517.3 3.6 gather_fusion.1
  520.9 4.4 convolution_bitcast_fusion.2
  531.5 5.3 bitcast_add_fusion.2
  537.0 3.6 gather_fusion.1
  540.6 4.4 convolution_bitcast_fusion.2
  551.2 5.3 bitcast_add_fusion.2
  556.5 4.1 fusion.6
  (195 shorter events, 126.3 us)
Async XLA Ops:
  6.5 235.3 %copy-start = (s32[24,1,2]{0,2,1:T(2,128)S(1)}, s32[24,1,2]{0,2,1:T(2,128)}, u32[]{:S(2)}) copy-start(s32[24,1,2]{0,2,1:T(2,128)} %param.11) | copy-start | bytes 580
  6.5 57.9 %all-gather.4.cloned.1.call-start = ((), (), s32[]{:S(2)}) async-start(), calls=%async_computation | async-start | bytes 7077888 | tf_op jit(solution)/shard_map/all_gather | solution.py:43
  7.3 234.6 %all-gather.6.cloned.1.call-start = ((), (), s32[]{:S(2)}) async-start(), calls=%async_computation.1 | async-start | bytes 25952256 | tf_op jit(solution)/shard_map/all_gather | solution.py:50
Sparse Core Ops, SparseCore 0:
  9.2 47.6 all-gather.3
  59.4 182.3 all-gather.5
where the time goes:
time: 569 us; the launch traced here: 567 us
  waiting for transfers between devices  179 us (31%)
  other arithmetic  136 us (24%)
  local copies, waits for them, and re-layouts  117 us (21%)
  matrix products  70.6 us (12%)
  blocking collectives  50.6 us (9%)
  between operations  14 us (2%)
    all_gather x1, waiting for transfers between devices, shards(): lax.all_gather(y_blocks, ('cols', 'layers'), axis=1, tiled=True)  177 us
    add x16, other arithmetic, advance(): return summed + weighted  83.7 us
    dot_general x16, matrix products, advance(): jnp.einsum('igab,igtbc->igtac', left_blocks, right_blocks, preferred_elem...  70.6 us
    gather x16, local copies, waits for them, and re-layouts, advance(): right_blocks = lookup[lookup_rows]  58.1 us
    reduce_sum x16, other arithmetic, advance(): jnp.sum(products[:, :, :, None] * present[..., None, None], axis=1)  43 us
    mul x16, local copies, waits for them, and re-layouts, advance(): products[:, :, :, None] * present[..., None, None]  38 us
    all_gather x1, blocking collectives, shards(): lax.all_gather(y_cols, ('cols', 'layers'), axis=1, tiled=True)  36.9 us
    unnamed x1, blocking collectives  13.6 us
  transfers between devices with their start and end apart: 2, of which 1 were waited for; matrix products, arithmetic and copies ran while one was open for 1% of the time, Pallas kernels for 0%

commit v1 on v0

--- a/solution.py
+++ b/solution.py
@@ -47,7 +47,15 @@
     summed = partial_products(
         initial,
         (
-            lax.all_gather(y_blocks, ("cols", "layers"), axis=1, tiled=True),
+            jnp.concatenate(
+                lax.all_to_all(
+                    jnp.stack([y_blocks] * lax.axis_size(("cols", "layers"))),
+                    ("cols", "layers"),
+                    0,
+                    0,
+                ),
+                axis=1,
+            ),
             lax.all_gather(y_cols, ("cols", "layers"), axis=1, tiled=True),
         ),
         lookup,

time: 569 us -> 996 us (1.75)
  blocking collectives: 50.6 us -> 635 us
  waiting for transfers between devices: 179 us -> 0.68 us
  starting transfers between devices: 0.04 us -> 12.2 us
    all_gather x1, blocking collectives: 36.9 us -> 620 us  [shards(): lax.all_gather(y_cols, ('cols', 'layers'), axis=1, tiled=True)]
    all_gather x1 -> x0, waiting for transfers between devices: 177 us -> none  [shards(): lax.all_gather(y_blocks, ('cols', 'layers'), axis=1, tiled=True)]
    all_to_all x0 -> x1, starting transfers between devices: none -> 12.1 us  [shards(): lax.all_to_all(jnp.stack([y_blocks] * lax.axis_size(('cols', 'layers'))),...]
  transfers between devices with their start and end apart: 2 -> 2, of which waited for: 1 -> 0; matrix products, arithmetic and copies ran while one was open for 1% -> 0% of each run, Pallas kernels for 0% -> 0%
where the time goes in v1:
time: 996 us; the launch traced here: 993 us
  blocking collectives  635 us (64%)
  other arithmetic  134 us (13%)
  local copies, waits for them, and re-layouts  125 us (13%)
  matrix products  70.4 us (7%)
  between operations  14.2 us (1%)
  starting transfers between devices  12.2 us (1%)
    all_gather x1, blocking collectives, shards(): lax.all_gather(y_cols, ('cols', 'layers'), axis=1, tiled=True)  620 us
    add x16, other arithmetic, advance(): return summed + weighted  84 us
    dot_general x16, matrix products, advance(): jnp.einsum('igab,igtbc->igtac', left_blocks, right_blocks, preferred_elem...  70.4 us
    gather x16, local copies, waits for them, and re-layouts, advance(): right_blocks = lookup[lookup_rows]  58.1 us
    reduce_sum x16, other arithmetic, advance(): jnp.sum(products[:, :, :, None] * present[..., None, None], axis=1)  42.9 us
    mul x16, local copies, waits for them, and re-layouts, advance(): products[:, :, :, None] * present[..., None, None]  38 us
  transfers between devices with their start and end apart: 2, of which 0 were waited for; matrix products, arithmetic and copies ran while one was open for 0% of the time, Pallas kernels for 0%

profile of v1, /device:TPU:1, one launch (start us, length us, event | category | flops | bytes accessed | tf_op | source)
XLA Modules:
  0.0 993.1 jit_solution(1739323771541842713)
XLA Ops:
  6.5 9.9 stack.2
  16.4 12.1 %all-to-all-start = ((bf16[32,24,1,128,128]{4,3,1,2,0:T(8,128)(2,1)}), bf16[32,24,1,128,128]{4,3,1,2,0:T(8,128)(2,1)}, u32[]{:S(2)}, u32[]{:S(2)}) async-start(bf16[32,24,1,128,128]{4,3,1,2,0:T(8,128)(2,1)} %stack.2), calls=%async_computation | async-start | bytes 50331648 | tf_op jit(solution)/shard_map/all_to_all | solution.py:51
  30.8 620.1 %all-gather = s32[32,1,24]{2,1,0:T(1,128)S(1)} all-gather(s32[1,1,24]{2,1,0:T(1,128)S(1)} %bitcast.57), channel_id=1, replica_groups=mesh['rows'=8,'cols'=8,'layers'=4] {'cols','layers'}, dimensions={0}, use_global_device_ids=true | all-gather | bytes 3168 | tf_op jit(solution)/shard_map/all_gather | solution.py:59
  651.0 15.1 %all-reduce = s32[192]{0:T(256)S(1)} all-reduce(s32[192]{0:T(256)S(1)} %bitcast_dynamic-update-slice_fusion), channel_id=1, replica_groups=mesh['rows'=8,'cols'=8,'layers'=4] {'rows'}, use_global_device_ids=true, to_apply=%add | all-reduce | flops 192 | bytes 1536
  667.5 314.6 %while.16 = (s32[]{:T(128)}, f32[24,1,2,128,128]{4,3,2,0,1:T(8,128)}, s32[24,32]{0,1:T(8,128)S(1)}, bf16[192,1,128,128]{3,2,1,0:T(8,128)(2,1)}, bf16[24,32,128,1...) while((s32[]{:T(128)}, ...), condition=%wide.region_2.3_spmd.clone, body=%wide.region_0.2_spmd.clone.sunk | while | flops 205260784 | bytes 31465964 | solution.py:34
  667.7 3.6 gather_fusion.1
  671.4 4.4 convolution_bitcast_fusion.2
  681.9 4.4 bitcast_add_fusion.2
  686.5 3.6 gather_fusion.1
  690.1 4.4 convolution_bitcast_fusion.2
  700.7 5.3 bitcast_add_fusion.2
  706.2 3.6 gather_fusion.1
  709.9 4.4 convolution_bitcast_fusion.2
  720.4 5.3 bitcast_add_fusion.2
  725.9 3.6 gather_fusion.1
  729.6 4.4 convolution_bitcast_fusion.2
  740.1 5.3 bitcast_add_fusion.2
  745.7 3.6 gather_fusion.1
  749.3 4.4 convolution_bitcast_fusion.2
  759.8 5.3 bitcast_add_fusion.2
  765.4 3.6 gather_fusion.1
  769.0 4.4 convolution_bitcast_fusion.2
  779.6 5.3 bitcast_add_fusion.2
  785.1 3.6 gather_fusion.1
  788.8 4.4 convolution_bitcast_fusion.2
  799.3 5.3 bitcast_add_fusion.2
  804.8 3.6 gather_fusion.1
  808.5 4.4 convolution_bitcast_fusion.2
  819.0 5.3 bitcast_add_fusion.2
  828.2 4.4 convolution_bitcast_fusion.2
  838.7 5.3 bitcast_add_fusion.2
  847.9 4.4 convolution_bitcast_fusion.2
  858.5 5.3 bitcast_add_fusion.2
  867.6 4.4 convolution_bitcast_fusion.2
  878.2 5.3 bitcast_add_fusion.2
  883.7 3.6 gather_fusion.1
  887.4 4.4 convolution_bitcast_fusion.2
  897.9 5.3 bitcast_add_fusion.2
  907.1 4.4 convolution_bitcast_fusion.2
  917.6 5.3 bitcast_add_fusion.2
  926.8 4.4 convolution_bitcast_fusion.2
  937.3 5.3 bitcast_add_fusion.2
  946.5 4.4 convolution_bitcast_fusion.2
  957.1 5.3 bitcast_add_fusion.2
  962.6 3.6 gather_fusion.1
  966.3 4.4 convolution_bitcast_fusion.2
  976.8 5.3 bitcast_add_fusion.2
  982.1 4.1 fusion.5
  (203 shorter events, 126.1 us)
Async XLA Ops:
  16.4 12.9 %copy-start.1 = (s32[24,1,2]{0,2,1:T(2,128)S(1)}, s32[24,1,2]{0,2,1:T(2,128)}, u32[]{:S(2)}) copy-start(s32[24,1,2]{0,2,1:T(2,128)} %param.11) | copy-start | bytes 580
  16.4 12.9 %copy-start.2 = (s32[24,1]{0,1:T(1,128)S(1)}, s32[24,1]{0,1:T(1,128)}, u32[]{:S(2)}) copy-start(s32[24,1]{0,1:T(1,128)} %param.8) | copy-start | bytes 292
  16.4 13.0 %copy-start.4 = (u32[256]{0:T(256)S(1)}, u32[256]{0:T(256)}, u32[]{:S(2)}) copy-start(u32[256]{0:T(256)} %constant.107) | copy-start | bytes 3076
  16.4 634.5 %copy-start.3 = (s32[24,1]{0,1:T(1,128)S(1)}, s32[24,1]{0,1:T(1,128)}, u32[]{:S(2)}) copy-start(s32[24,1]{0,1:T(1,128)} %param.10) | copy-start | bytes 292
  16.4 649.7 %copy-start = (bf16[24,1,128,128]{3,2,1,0:T(8,128)(2,1)S(1)}, bf16[24,1,128,128]{3,2,1,0:T(8,128)(2,1)}, u32[]{:S(2)}) copy-start(bf16[24,1,128,128]{3,2,1,0:T(8,128)(2,1)} %param.7) | copy-start | bytes 2359300
  16.4 651.0 %all-to-all-start = ((bf16[32,24,1,128,128]{4,3,1,2,0:T(8,128)(2,1)}), bf16[32,24,1,128,128]{4,3,1,2,0:T(8,128)(2,1)}, u32[]{:S(2)}, u32[]{:S(2)}) async-start(bf16[32,24,1,128,128]{4,3,1,2,0:T(8,128)(2,1)} %stack.2), calls=%async_computation | async-start | bytes 50331648 | tf_op jit(solution)/shard_map/all_to_all | solution.py:51
  28.6 638.9 %all-gather.3.cloned.1.call-start = ((), (), s32[]{:S(2)}) async-start(), calls=%async_computation.1 | async-start | bytes 7077888 | tf_op jit(solution)/shard_map/all_gather | solution.py:43
Sparse Core Ops, SparseCore 0:
  31.2 45.4 all-gather.2
